TPU v7x, 512 devices: a whole 4x4x16 slice. The times are simulated.
512 devices in a mesh: sec: 2 (over core), seq: 32 (over z, y_lo), rep: 8 (over x, y_hi).
Axes of the slice: x: 4, y: 4 (y_hi: 2, y_lo: 2; y = y_hi * 2 + y_lo), z: 16, core: 2. Of those that a mesh axis runs over, the one named last changes fastest.
Arguments:
- head_query: bfloat16 [64, 24, 1536, 128], P(('sec', 'rep'), None, 'seq'), may hold values from -4.5 to 4.5
- head_keys: bfloat16 [64, 24, 1536, 128], P(('sec', 'rep'), None, 'seq'), may hold values from -4.5 to 4.5
- head_values: bfloat16 [64, 24, 1536, 128], P(('sec', 'rep'), None, 'seq'), may hold values from -6 to 6
- mod_shift: float32 [64, 3072], P(('sec', 'rep')), may hold values from -3 to 3
- mod_scale: float32 [64, 3072], P(('sec', 'rep')), may hold values from -0.9 to 0.9
- final_weight: bfloat16 [3072, 64], replicated, may hold values from -0.109375 to 0.109375
- final_bias: float32 [64], replicated, may hold values from -3 to 3
- noisy_latent: float32 [64, 3, 64, 512], P(('sec', 'rep'), None, 'seq'), may hold values from -7.2 to 7.2
- step_index: int32 [64], P(('sec', 'rep')), may hold values from 46 to 49
- clip_order: int32 [64], replicated, may hold values from 0 to 63, each once
- conv_weight: bfloat16 [3, 3, 3, 16, 512], replicated, may hold values from -0.3125 to 0.3125
- conv_bias: float32 [512], replicated, may hold values from -3 to 3
- group_gain: float32 [512], replicated, may hold values from 0.1 to 1.9
- group_shift: float32 [512], replicated, may hold values from -3 to 3
Outputs:
- denoised: float32 [64, 3, 64, 512], P(('sec', 'rep'), None, 'seq')
- features: bfloat16 [64, 3, 64, 16384], P(('sec', 'rep'), None, 'seq')
All inputs are finite; a program needn't handle non-finite values.
Results may differ from a plain program's by a relative error of at most 0.005.
Values may be sent and summed in bfloat16 or wider, within the bound.
No kernel may reach another device: no remote copies, remote signals or barrier semaphores. Data moves between devices by JAX's collectives and lax.ppermute only.
A program may use at most 128 MiB of HBM per device.

v0:
```python
import math
import jax
import jax.numpy as jnp
from jax import lax
from jax.sharding import PartitionSpec as P

HEADS = 24
HEAD_DIM = 128
LAT_CH = 16
VAE_CH = 512
GROUPS = 32
FRAMES = 3
PATCH_W = 16
NSTEPS = 50
PATCH_OUT = 64
LAT_W = 32
eps_norm = 1e-06
shift_factor = 7.0


def extended(cells, sides, width):
    for axis, dim in sides:
        count = lax.axis_size(axis)
        ends = count - 1
        head = lax.slice_in_dim(cells, 0, width, axis=dim)
        tail = lax.slice_in_dim(cells, cells.shape[dim] - width, cells.shape[dim], axis=dim)
        cells = jnp.concatenate(
            [
                lax.ppermute(tail, axis, [(i, (i + 1) % count) for i in range(ends)]),
                cells,
                lax.ppermute(head, axis, [((i + 1) % count, i) for i in range(ends)]),
            ],
            axis=dim,
        )
    return cells


def attend_unit(operands):
    query_rows, key_rows, value_rows = operands
    length = query_rows.shape[0]
    block = math.gcd(length, 512)
    scale = 1.0 / math.sqrt(query_rows.shape[1])
    blocks = query_rows.reshape(length // block, block, query_rows.shape[1])

    def one_block(rows):
        scores = jnp.dot(rows, key_rows.T, preferred_element_type=jnp.float32) * scale
        top = jnp.max(scores, axis=1, keepdims=True)
        expd = jnp.exp(scores - top)
        weights = (expd / jnp.sum(expd, axis=1, keepdims=True)).astype(jnp.bfloat16)
        return jnp.dot(weights, value_rows, preferred_element_type=jnp.float32).astype(jnp.bfloat16)

    return lax.map(one_block, blocks).reshape(length, query_rows.shape[1])


def sigma_level(index):
    level = 1.0 - index.astype(jnp.float32) / NSTEPS
    return shift_factor * level / (1.0 + (shift_factor - 1.0) * level)


def causal_columns(rimmed):
    clips, frames, rows_rim, wide = rimmed.shape
    width = wide // LAT_CH
    grid = rimmed.reshape(clips, frames, rows_rim, width, LAT_CH)
    first = grid[:, :1]
    grid = jnp.concatenate([first, first, grid], axis=1)
    grid = jnp.pad(grid, ((0, 0), (0, 0), (0, 0), (1, 1), (0, 0)), mode="edge")
    taps = []
    for tap_time in range(3):
        for tap_row in range(3):
            for tap_col in range(3):
                taps.append(
                    grid[
                        :,
                        tap_time : tap_time + frames,
                        tap_row : tap_row + rows_rim - 2,
                        tap_col : tap_col + width,
                        :,
                    ]
                )
    return jnp.stack(taps, axis=4).reshape(clips, frames, rows_rim - 2, width, 27 * LAT_CH)


def edge_rows(rimmed):
    position = lax.axis_index("seq")
    last_index = lax.axis_size("seq") - 1
    upper = jnp.where(position == 0, rimmed[:, :, 1:2], rimmed[:, :, 0:1])
    lower = jnp.where(position == last_index, rimmed[:, :, -2:-1], rimmed[:, :, -1:])
    return jnp.concatenate([upper, rimmed[:, :, 1:-1], lower], axis=2)


def shards(
    head_query,
    head_keys,
    head_values,
    mod_shift,
    mod_scale,
    final_weight,
    final_bias,
    noisy_latent,
    step_index,
    clip_order,
    conv_weight,
    conv_bias,
    group_gain,
    group_shift,
):
    n_seq = lax.axis_size("seq")
    clips = head_query.shape[0]
    tok_dev = head_query.shape[2]
    units_local = clips * HEADS // n_seq
    query_four = head_query.reshape(n_seq, units_local, tok_dev, HEAD_DIM)
    keys_four = head_keys.reshape(n_seq, units_local, tok_dev, HEAD_DIM)
    values_four = head_values.reshape(n_seq, units_local, tok_dev, HEAD_DIM)
    query_part = lax.all_to_all(query_four, "seq", split_axis=0, concat_axis=2, tiled=True)
    keys_part = lax.all_to_all(keys_four, "seq", split_axis=0, concat_axis=2, tiled=True)
    values_part = lax.all_to_all(values_four, "seq", split_axis=0, concat_axis=2, tiled=True)
    outputs = lax.map(attend_unit, (query_part[0], keys_part[0], values_part[0]))[None]
    mixed = lax.all_to_all(outputs, "seq", split_axis=2, concat_axis=0, tiled=True)
    weights3 = final_weight.astype(jnp.float32).reshape(HEADS, HEAD_DIM, PATCH_OUT)
    scale3 = mod_scale.reshape(clips, HEADS, HEAD_DIM)
    shift3 = mod_shift.reshape(clips, HEADS, HEAD_DIM)
    heads = mixed.reshape(clips, HEADS, tok_dev, HEAD_DIM).astype(jnp.float32)
    mean = jnp.mean(heads, axis=(1, 3), keepdims=True)
    spread = jnp.mean(jnp.square(heads - mean), axis=(1, 3), keepdims=True)
    normed = (heads - mean) * lax.rsqrt(spread + eps_norm)
    modulated = normed * (1.0 + scale3[:, :, None, :]) + shift3[:, :, None, :]
    velocity = (
        jnp.einsum("chtd,hdo->cto", modulated, weights3, precision=lax.Precision.HIGHEST)
        + final_bias
    )
    rows_dev = noisy_latent.shape[2]
    velocity = velocity.reshape(clips, rows_dev // 2, FRAMES, PATCH_W, 2, 2, LAT_CH)
    velocity = jnp.transpose(velocity, (0, 2, 1, 4, 3, 5, 6)).reshape(noisy_latent.shape)
    step = sigma_level(step_index + 1) - sigma_level(step_index)
    denoised = noisy_latent + step[:, None, None, None] * velocity
    decoder_in = denoised.astype(jnp.bfloat16)
    group_index = lax.axis_index(("sec", "rep"))
    wanted = lax.dynamic_slice_in_dim(clip_order, group_index * clips, clips)
    everyone = lax.all_gather(decoder_in, ("sec", "rep"), axis=0, tiled=True)
    picked = jnp.take(everyone, wanted, axis=0)
    rimmed = edge_rows(extended(picked, (("seq", 2),), 1))
    columns = causal_columns(rimmed)
    flat_weight = conv_weight.reshape(27 * LAT_CH, VAE_CH)
    conv_out = (
        jnp.dot(columns.reshape(-1, 27 * LAT_CH), flat_weight, preferred_element_type=jnp.float32)
        + conv_bias
    )
    conv_out = conv_out.reshape(clips, -1, GROUPS, VAE_CH // GROUPS)
    cells = conv_out.shape[1] * n_seq * (VAE_CH // GROUPS)
    local_sum = jnp.sum(conv_out, axis=(1, 3))
    mean = lax.psum(local_sum, "seq") / cells
    centered = conv_out - mean[:, None, :, None]
    spread = lax.psum(jnp.sum(jnp.square(centered), axis=(1, 3)), "seq") / cells
    normed = (centered * lax.rsqrt(spread + eps_norm)[:, None, :, None]).reshape(clips, -1, VAE_CH)
    features = jax.nn.silu(normed * group_gain + group_shift).astype(jnp.bfloat16)
    features = features.reshape(clips, FRAMES, rows_dev, LAT_W * VAE_CH)
    return (denoised, features)


def solution(mesh):
    placed = (
        P(("sec", "rep"), None, "seq", None),
        P(("sec", "rep"), None, "seq", None),
        P(("sec", "rep"), None, "seq", None),
        P(("sec", "rep"), None),
        P(("sec", "rep"), None),
        P(),
        P(),
        P(("sec", "rep"), None, "seq", None),
        P(("sec", "rep")),
        P(),
        P(),
        P(),
        P(),
        P(),
    )
    return jax.shard_map(
        shards,
        mesh=mesh,
        in_specs=placed,
        out_specs=(P(("sec", "rep"), None, "seq", None), P(("sec", "rep"), None, "seq", None)),
        check_vma=False,
    )
```

profile of v0, /device:TPU:8, one launch (start us, length us, event | category | flops | bytes accessed | tf_op | source)
XLA Modules:
  0.0 569.3 jit_solution(6883211467850710125)
XLA Ops:
  0.7 77.9 %all_to_all.54 = bf16[32,3,48,128]{3,2,1,0:T(8,128)(2,1)} all-to-all(bf16[32,3,48,128]{3,2,1,0:T(8,128)(2,1)} %bitcast.227), channel_id=1, replica_groups=mesh['sec'=2,'seq'=32,'rep'=8] {'seq'}, dimensions={0} | all-to-all | bytes 2359296 | tf_op jit(solution)/shard_map/all_to_all | solution.py:114
  78.5 64.2 %all_to_all.55 = bf16[32,3,48,128]{3,2,1,0:T(8,128)(2,1)} all-to-all(bf16[32,3,48,128]{3,2,1,0:T(8,128)(2,1)S(1)} %bitcast.228), channel_id=1, replica_groups=mesh['sec'=2,'seq'=32,'rep'=8] {'seq'}, dimensions={0} | all-to-all | bytes 2359296 | tf_op jit(solution)/shard_map/all_to_all | solution.py:115
  142.7 4.2 all-to-all-start.2
  146.9 1.4 copy.116
  148.5 1.1 copy.117
  149.6 55.0 %all-to-all-done.2 = bf16[32,3,48,128]{3,2,1,0:T(8,128)(2,1)S(1)} async-done(((bf16[32,3,48,128]{3,2,1,0:T(8,128)(2,1)}), bf16[32,3,48,128]{3,2,1,0:T(8,128)(2,1)S(1)}, u32[]{:S(2)}, u32[]{:S(2)}) %all-to-all-start.2) | async-done | bytes 1179680 | tf_op jit(solution)/shard_map/all_to_all | solution.py:116
  204.6 1.1 copy.118
  205.8 24.2 %while.21 = (s32[]{:T(128)}, bf16[3,1536,128]{2,1,0:T(8,128)(2,1)}, bf16[3,1536,128]{2,1,0:T(8,128)(2,1)S(1)}, bf16[3,1536,128]{2,1,0:T(8,128)(2,1)}, bf16[3,153...) while((s32[]{:T(128)}, bf16[3,1536,128]{2,1,0:T(8,128)(2,1)}, ...), condition=%wide.region_5.6_spmd, body=%wide.region_0.5_spmd.sunk | while | flops 408222720 | bytes 13641974 | solution.py:117
  205.8 1.2 dynamic-slice_bitcast_fusion.3
  207.0 6.1 %while.22 = (s32[]{:T(128)}, bf16[3,512,128]{2,1,0:T(8,128)(2,1)S(1)}, bf16[3,512,128]{2,1,0:T(8,128)(2,1)S(1)}, bf16[1536,128]{1,0:T(8,128)(2,1)S(1)}, bf16[1536,128]{1,0:T(8,128)(2,1)S(1)}, /*index=5*/s32[]{:T(128)}) while((s32[]{:T(128)}, bf16[3,512,128]{2,1,0:T(8,128)(2,1)S(1)}, bf16[3,512,128]{2,1,0:T(8,128)(2,1)S(1)}, ...), condition=%wide.region_4.4_spmd, body=%wide.region_1.3_spmd.sunk | while | flops 408222720 | bytes 10496085 | solution.py:52
  208.2 0.8 fusion.89
  210.2 0.8 fusion.89
  212.2 0.8 fusion.89
  213.0 0.8 bitcast_dynamic-update-slice_fusion.2
  213.8 1.2 dynamic-slice_bitcast_fusion.3
  215.0 6.1 %while.22 = (s32[]{:T(128)}, bf16[3,512,128]{2,1,0:T(8,128)(2,1)S(1)}, bf16[3,512,128]{2,1,0:T(8,128)(2,1)S(1)}, bf16[1536,128]{1,0:T(8,128)(2,1)S(1)}, bf16[1536,128]{1,0:T(8,128)(2,1)S(1)}, /*index=5*/s32[]{:T(128)}) while((s32[]{:T(128)}, bf16[3,512,128]{2,1,0:T(8,128)(2,1)S(1)}, bf16[3,512,128]{2,1,0:T(8,128)(2,1)S(1)}, ...), condition=%wide.region_4.4_spmd, body=%wide.region_1.3_spmd.sunk | while | flops 408222720 | bytes 10496085 | solution.py:52
  216.3 0.8 fusion.89
  218.3 0.8 fusion.89
  220.3 0.8 fusion.89
  221.1 0.8 bitcast_dynamic-update-slice_fusion.2
  221.9 1.2 dynamic-slice_bitcast_fusion.3
  223.1 6.1 %while.22 = (s32[]{:T(128)}, bf16[3,512,128]{2,1,0:T(8,128)(2,1)S(1)}, bf16[3,512,128]{2,1,0:T(8,128)(2,1)S(1)}, bf16[1536,128]{1,0:T(8,128)(2,1)S(1)}, bf16[1536,128]{1,0:T(8,128)(2,1)S(1)}, /*index=5*/s32[]{:T(128)}) while((s32[]{:T(128)}, bf16[3,512,128]{2,1,0:T(8,128)(2,1)S(1)}, bf16[3,512,128]{2,1,0:T(8,128)(2,1)S(1)}, ...), condition=%wide.region_4.4_spmd, body=%wide.region_1.3_spmd.sunk | while | flops 408222720 | bytes 10496085 | solution.py:52
  224.3 0.8 fusion.89
  226.3 0.8 fusion.89
  228.4 0.8 fusion.89
  229.1 0.8 bitcast_dynamic-update-slice_fusion.2
  229.9 8.1 %copy.141 = bf16[3,1536,128]{2,0,1:T(4,128)(2,1)} copy(bf16[3,1536,128]{2,1,0:T(8,128)(2,1)} %get-tuple-element.56) | data formatting | bytes 2359296 | tf_op jit(solution)/shard_map/while | solution.py:117
  238.1 5.7 all-to-all-start.3
  243.9 76.1 %all-to-all-done.3 = bf16[1,3,1536,128]{3,1,0,2:T(4,128)(2,1)S(1)} async-done(((bf16[1,3,1536,128]{3,1,0,2:T(4,128)(2,1)}), bf16[1,3,1536,128]{3,1,0,2:T(4,128)(2,1)S(1)}, u32[]{:S(2)}, u32[]{:S(2)}) %all-to-all-start.3) | async-done | bytes 1179680 | tf_op jit(solution)/shard_map/all_to_all | solution.py:118
  320.4 3.1 fusion.19
  323.7 22.0 %multiply_reduce_fusion = f32[32,48]{1,0:T(8,128)S(1)} fusion(bf16[1,3,32,48,128]{4,1,3,2,0:T(4,128)(2,1)S(1)} %bitcast.219, f32[32,48]{1,0:T(8,128)S(1)} %broadcast_bitcast_fusion.2), kind=kLoop, calls=%fused_computation.17 | loop fusion | flops 2357760 | bytes 1191936 | tf_op jit(solution)/shard_map/reduce_sum | solution.py:124
  345.8 1.6 fusion.28
  348.4 0.7 fusion.72
  349.2 36.8 %all_gather.3 = bf16[64,3,2,512]{3,2,1,0:T(2,128)(2,1)S(1)} all-gather(bf16[4,3,2,512]{3,2,1,0:T(2,128)(2,1)S(1)} %get-tuple-element.79), channel_id=1, replica_groups=mesh['sec'=2,'seq'=32,'rep'=8] {'sec','rep'}, dimensions={0}, use_global_device_ids=true | all-gather | bytes 417792 | tf_op jit(solution)/shard_map/all_gather | solution.py:139
  386.7 3.1 collective-permute-start
  389.8 3.0 collective-permute-start.1
  392.8 3.5 collective-permute-done.1
  398.7 0.7 fusion.69
  400.1 0.7 fusion.67
  400.9 0.7 fusion.66
  402.3 0.7 fusion.40
  403.0 0.7 fusion.64
  404.4 0.7 fusion.48
  405.1 0.7 fusion.62
  406.6 0.7 fusion.45
  407.3 0.7 fusion.60
  408.0 0.7 fusion.59
  408.7 0.7 fusion.42
  409.4 0.7 fusion.58
  411.6 0.7 fusion.55
  413.7 0.7 fusion.52
  415.8 0.7 fusion.49
  416.5 7.9 %copy.123 = bf16[4,3,2,32,27,16]{3,2,1,0,5,4:T(2,128)(2,1)S(1)} copy(bf16[4,3,2,32,27,16]{5,3,2,1,0,4:T(8,128)(2,1)} %fusion.49) | data formatting | bytes 1327104 | tf_op jit(solution)/shard_map/stack | solution.py:80
  424.5 2.5 reshape_reshape.3
  427.0 1.7 convolution_add_fusion
  428.7 1.6 copy.124
  430.3 2.5 reshape.109
  432.8 2.7 reshape.110
  436.0 59.9 %psum.14 = f32[4,32]{1,0:T(4,128)S(1)} all-reduce(f32[4,32]{1,0:T(4,128)S(1)} %copy.125), channel_id=1, replica_groups=mesh['sec'=2,'seq'=32,'rep'=8] {'seq'}, use_global_device_ids=true, to_apply=%region_11.12 | all-reduce | flops 128 | bytes 1024 | tf_op jit(solution)/shard_map/psum | solution.py:151
  496.0 0.8 multiply_reduce_fusion.1
  496.8 62.3 %psum.15 = f32[4,32]{1,0:T(4,128)S(1)} all-reduce(f32[4,32]{1,0:T(4,128)S(1)} %copy.127), channel_id=1, replica_groups=mesh['sec'=2,'seq'=32,'rep'=8] {'seq'}, use_global_device_ids=true, to_apply=%region_13.14 | all-reduce | flops 128 | bytes 1024 | tf_op jit(solution)/shard_map/psum | solution.py:153
  559.5 2.5 mul.94
  562.3 2.5 sub.70
  564.8 4.5 fusion.20
  (104 shorter events, 24.5 us)
Async XLA Ops:
  0.6 426.3 %copy-start = (bf16[3,3,3,16,512]{4,3,2,1,0:T(8,128)(2,1)S(1)}, bf16[3,3,3,16,512]{4,3,2,1,0:T(8,128)(2,1)}, u32[]{:S(2)}) copy-start(bf16[3,3,3,16,512]{4,3,2,1,0:T(8,128)(2,1)} %param.28) | copy-start | bytes 1327108
  0.6 77.9 %copy-start.2 = (bf16[4,24,48,128]{3,2,1,0:T(8,128)(2,1)S(1)}, bf16[4,24,48,128]{3,2,1,0:T(8,128)(2,1)}, u32[]{:S(2)}) copy-start(bf16[4,24,48,128]{3,2,1,0:T(8,128)(2,1)} %param.19) | copy-start | bytes 3538948
  142.7 61.9 %all-to-all-start.2 = ((bf16[32,3,48,128]{3,2,1,0:T(8,128)(2,1)}), bf16[32,3,48,128]{3,2,1,0:T(8,128)(2,1)S(1)}, u32[]{:S(2)}, u32[]{:S(2)}) async-start(bf16[32,3,48,128]{3,2,1,0:T(8,128)(2,1)} %bitcast.14), calls=%async_computation.2 | async-start | bytes 2359296 | tf_op jit(solution)/shard_map/all_to_all | solution.py:116
  146.9 1.6 copy-start.1
  229.9 13.8 %copy-start.8 = (s32[64]{0:T(128)S(1)}, s32[64]{0:T(128)}, u32[]{:S(2)}) copy-start(s32[64]{0:T(128)} %param.27) | copy-start | bytes 772
  229.9 13.9 %copy-start.11 = (s32[4]{0:T(128)S(1)}, s32[4]{0:T(128)}, u32[]{:S(2)}) copy-start(s32[4]{0:T(128)} %param.26) | copy-start | bytes 52
  229.9 13.9 %copy-start.6 = (f32[512]{0:T(512)S(1)}, f32[512]{0:T(512)}, u32[]{:S(2)}) copy-start(f32[512]{0:T(512)} %param.31) | copy-start | bytes 6148
  229.9 14.0 %copy-start.3 = (f32[4,3072]{1,0:T(4,128)S(1)}, f32[4,3072]{1,0:T(4,128)}, u32[]{:S(2)}) copy-start(f32[4,3072]{1,0:T(4,128)} %param.22) | copy-start | bytes 147460
  229.9 14.0 %copy-start.4 = (f32[4,3072]{1,0:T(4,128)S(1)}, f32[4,3072]{1,0:T(4,128)}, u32[]{:S(2)}) copy-start(f32[4,3072]{1,0:T(4,128)} %param.21) | copy-start | bytes 147460
  238.1 82.0 %all-to-all-start.3 = ((bf16[1,3,1536,128]{3,1,0,2:T(4,128)(2,1)}), bf16[1,3,1536,128]{3,1,0,2:T(4,128)(2,1)S(1)}, u32[]{:S(2)}, u32[]{:S(2)}) async-start(bf16[1,3,1536,128]{3,1,0,2:T(4,128)(2,1)} %bitcast.224), calls=%async_computation.3 | async-start | bytes 3145728 | tf_op jit(solution)/shard_map/all_to_all | solution.py:118
  323.5 22.3 %copy-start.9 = (bf16[3072,64]{0,1:T(8,128)(2,1)S(1)}, bf16[3072,64]{0,1:T(8,128)(2,1)}, u32[]{:S(2)}) copy-start(bf16[3072,64]{0,1:T(8,128)(2,1)} %param.23) | copy-start | bytes 1179652
  323.5 22.3 %copy-start.12 = (f32[64]{0:T(128)S(1)}, f32[64]{0:T(128)}, u32[]{:S(2)}) copy-start(f32[64]{0:T(128)} %param.24) | copy-start | bytes 772
  323.7 24.7 %copy-start.5 = (f32[4,3,2,512]{3,2,1,0:T(2,128)S(1)}, f32[4,3,2,512]{3,2,1,0:T(2,128)}, u32[]{:S(2)}) copy-start(f32[4,3,2,512]{3,2,1,0:T(2,128)} %param.25) | copy-start | bytes 147460
  345.8 47.0 %copy-start.7 = (f32[512]{0:T(512)S(1)}, f32[512]{0:T(512)}, u32[]{:S(2)}) copy-start(f32[512]{0:T(512)} %param.30) | copy-start | bytes 6148
  386.7 6.2 %collective-permute-start = (bf16[4,3,1,512]{3,2,1,0:T(2,128)(2,1)S(1)}, bf16[4,3,1,512]{3,2,1,0:T(2,128)(2,1)S(1)}, u32[]{:S(2)}, u32[]{:S(2)}) collective-permute-start(bf16[4,3,1,512]{3,2,1,0:T(2,128)(2,1)S(1)} %get-tuple-element.89), channel_id=1, source_target_pairs={{0,8},{8,16},{16,24},{24,32},{32,40},{40,48},{48,56},{56,64},{64,7... | collective-permute-start | bytes 36872 | tf_op jit(solution)/shard_map/ppermute | solution.py:29
  389.8 6.6 %collective-permute-start.1 = (bf16[4,3,1,512]{3,2,1,0:T(2,128)(2,1)S(1)}, bf16[4,3,1,512]{3,2,1,0:T(2,128)(2,1)S(1)}, u32[]{:S(2)}, u32[]{:S(2)}) collective-permute-start(bf16[4,3,1,512]{3,2,1,0:T(2,128)(2,1)S(1)} %get-tuple-element.90), channel_id=1, source_target_pairs={{8,0},{16,8},{24,16},{32,24},{40,32},{48,40},{56,48},{64,56},{72,6... | collective-permute-start | bytes 36872 | tf_op jit(solution)/shard_map/ppermute | solution.py:31
  424.4 2.5 copy-start.10
where the time goes:
time: 570 us; the launch traced here: 569 us
  blocking collectives  301 us (53%)
  waiting for transfers between devices  135 us (24%)
  local copies, waits for them, and re-layouts  58.9 us (10%)
  other arithmetic  41.5 us (7%)
  matrix products  16.1 us (3%)
  starting transfers between devices  15.9 us (3%)
    all_to_all x1, blocking collectives, shards(): lax.all_to_all(query_four, 'seq', split_axis=0, concat_axis=2, tiled=True)  77.9 us
    all_to_all x1, waiting for transfers between devices, shards(): lax.all_to_all(outputs, 'seq', split_axis=2, concat_axis=0, tiled=True)  76.1 us
    all_to_all x1, blocking collectives, shards(): lax.all_to_all(keys_four, 'seq', split_axis=0, concat_axis=2, tiled=True)  64.2 us
    psum x1, blocking collectives, shards(): spread = lax.psum(jnp.sum(jnp.square(centered), axis=(1, 3)), 'seq') / cells  62.3 us
    psum x1, blocking collectives, shards(): mean = lax.psum(local_sum, 'seq') / cells  59.9 us
    all_to_all x1, waiting for transfers between devices, shards(): lax.all_to_all(values_four, 'seq', split_axis=0, concat_axis=2, tiled=True)  55 us
    all_gather x1, blocking collectives, shards(): everyone = lax.all_gather(decoder_in, ('sec', 'rep'), axis=0, tiled=True)  36.8 us
    reduce_sum x2, other arithmetic, shards(): spread = jnp.mean(jnp.square(heads - mean), axis=(1, 3), keepdims=True)  22 us
  transfers between devices with their start and end apart: 4, of which 3 were waited for; matrix products, arithmetic and copies ran while one was open for 0% of the time, Pallas kernels for 0%

commit v1 on v0

--- a/solution.py
+++ b/solution.py
@@ -112,7 +112,10 @@
     keys_four = head_keys.reshape(n_seq, units_local, tok_dev, HEAD_DIM)
     values_four = head_values.reshape(n_seq, units_local, tok_dev, HEAD_DIM)
     query_part = lax.all_to_all(query_four, "seq", split_axis=0, concat_axis=2, tiled=True)
-    keys_part = lax.all_to_all(keys_four, "seq", split_axis=0, concat_axis=2, tiled=True)
+    keys_part = jnp.concatenate(
+        lax.all_to_all(jnp.stack(jnp.split(keys_four, lax.axis_size("seq"), axis=0)), "seq", 0, 0),
+        axis=2,
+    )
     values_part = lax.all_to_all(values_four, "seq", split_axis=0, concat_axis=2, tiled=True)
     outputs = lax.map(attend_unit, (query_part[0], keys_part[0], values_part[0]))[None]
     mixed = lax.all_to_all(outputs, "seq", split_axis=2, concat_axis=0, tiled=True)

time: 570 us -> 574 us (level)
  the two profiles are of different devices: /device:TPU:8 before, /device:TPU:6 now
where the time goes in v1:
time: 574 us; the launch traced here: 571 us
  blocking collectives  225 us (39%)
  waiting for transfers between devices  169 us (29%)
  local copies, waits for them, and re-layouts  84.7 us (15%)
  other arithmetic  41.5 us (7%)
  starting transfers between devices  33.4 us (6%)
  matrix products  16.1 us (3%)
    all_to_all x1, waiting for transfers between devices, shards(): lax.all_to_all(outputs, 'seq', split_axis=2, concat_axis=0, tiled=True)  74.3 us
    all_to_all x1, blocking collectives, shards(): lax.all_to_all(jnp.stack(jnp.split(keys_four, lax.axis_size('seq'), axis=...  66.3 us
    psum x1, blocking collectives, shards(): mean = lax.psum(local_sum, 'seq') / cells  61.4 us
    psum x1, blocking collectives, shards(): spread = lax.psum(jnp.sum(jnp.square(centered), axis=(1, 3)), 'seq') / cells  60.8 us
    all_to_all x1, waiting for transfers between devices, shards(): lax.all_to_all(values_four, 'seq', split_axis=0, concat_axis=2, tiled=True)  55.9 us
    unnamed x78, local copies, waits for them, and re-layouts  39 us
    all_gather x1, blocking collectives, shards(): everyone = lax.all_gather(decoder_in, ('sec', 'rep'), axis=0, tiled=True)  37 us
    all_to_all x1, waiting for transfers between devices, shards(): lax.all_to_all(query_four, 'seq', split_axis=0, concat_axis=2, tiled=True)  34.2 us
  transfers between devices with their start and end apart: 5, of which 4 were waited for; matrix products, arithmetic and copies ran while one was open for 5% of the time, Pallas kernels for 0%

profile of v1, /device:TPU:6, one launch (start us, length us, event | category | flops | bytes accessed | tf_op | source)
XLA Modules:
  0.0 571.0 jit_solution(17472371444419194063)
XLA Ops:
  0.6 16.6 %all-to-all-start = ((bf16[32,3,48,128]{3,2,1,0:T(8,128)(2,1)}), bf16[32,3,48,128]{3,2,1,0:T(8,128)(2,1)S(1)}, u32[]{:S(2)}, u32[]{:S(2)}) async-start(bf16[32,3,48,128]{3,2,1,0:T(8,128)(2,1)} %bitcast.385), calls=%async_computation | async-start | bytes 2359296 | tf_op jit(solution)/shard_map/all_to_all | solution.py:114
  18.1 0.8 constant_dynamic-update-slice_fusion.30
  18.8 0.8 constant_dynamic-update-slice_fusion.29
  19.6 0.8 constant_dynamic-update-slice_fusion.28
  20.4 0.8 constant_dynamic-update-slice_fusion.27
  21.2 0.8 constant_dynamic-update-slice_fusion.26
  21.9 0.8 constant_dynamic-update-slice_fusion.25
  22.7 0.8 constant_dynamic-update-slice_fusion.24
  23.5 0.8 constant_dynamic-update-slice_fusion.23
  24.3 0.8 constant_dynamic-update-slice_fusion.22
  25.1 0.8 constant_dynamic-update-slice_fusion.21
  25.8 0.8 constant_dynamic-update-slice_fusion.20
  26.6 0.8 constant_dynamic-update-slice_fusion.19
  27.4 0.8 constant_dynamic-update-slice_fusion.18
  28.2 0.8 constant_dynamic-update-slice_fusion.17
  28.9 0.8 constant_dynamic-update-slice_fusion.16
  29.7 0.8 constant_dynamic-update-slice_fusion.15
  30.5 0.8 constant_dynamic-update-slice_fusion.14
  32.0 0.8 constant_dynamic-update-slice_fusion.12
  32.8 0.8 constant_dynamic-update-slice_fusion.11
  33.6 0.8 constant_dynamic-update-slice_fusion.10
  34.4 0.8 constant_dynamic-update-slice_fusion.9
  35.2 0.8 constant_dynamic-update-slice_fusion.8
  35.9 0.8 constant_dynamic-update-slice_fusion.7
  36.7 0.8 constant_dynamic-update-slice_fusion.6
  39.0 0.8 constant_dynamic-update-slice_fusion.3
  39.8 0.8 constant_dynamic-update-slice_fusion.2
  40.6 0.8 constant_dynamic-update-slice_fusion.1
  41.4 0.8 constant_dynamic-update-slice_fusion
  42.1 34.2 %all-to-all-done = bf16[32,3,48,128]{3,2,1,0:T(8,128)(2,1)S(1)} async-done(((bf16[32,3,48,128]{3,2,1,0:T(8,128)(2,1)}), bf16[32,3,48,128]{3,2,1,0:T(8,128)(2,1)S(1)}, u32[]{:S(2)}, u32[]{:S(2)}) %all-to-all-start) | async-done | bytes 1179680 | tf_op jit(solution)/shard_map/all_to_all | solution.py:114
  76.4 66.3 %all_to_all.44 = bf16[32,1,3,48,128]{4,3,2,1,0:T(8,128)(2,1)} all-to-all(bf16[32,1,3,48,128]{4,3,2,1,0:T(8,128)(2,1)S(1)} %constant_dynamic-update-slice_fusion), channel_id=1, replica_groups=mesh['sec'=2,'seq'=32,'rep'=8] {'seq'}, dimensions={0} | all-to-all | bytes 2359296 | tf_op jit(solution)/shard_map/all_to_all | solution.py:116
  142.7 4.7 all-to-all-start.2
  147.4 2.4 copy.177
  149.8 55.9 %all-to-all-done.2 = bf16[32,3,48,128]{3,2,1,0:T(8,128)(2,1)} async-done(((bf16[32,3,48,128]{3,2,1,0:T(8,128)(2,1)}), bf16[32,3,48,128]{3,2,1,0:T(8,128)(2,1)}, u32[]{:S(2)}, u32[]{:S(2)}) %all-to-all-start.2) | async-done | bytes 1179680 | tf_op jit(solution)/shard_map/all_to_all | solution.py:119
  205.6 2.4 copy.178
  208.0 24.2 %while.21 = (s32[]{:T(128)}, bf16[3,1536,128]{2,1,0:T(8,128)(2,1)}, bf16[3,1536,128]{2,1,0:T(8,128)(2,1)S(1)}, bf16[3,1536,128]{2,1,0:T(8,128)(2,1)}, bf16[3,153...) while((s32[]{:T(128)}, bf16[3,1536,128]{2,1,0:T(8,128)(2,1)}, ...), condition=%wide.region_5.6_spmd, body=%wide.region_0.5_spmd.sunk | while | flops 408222720 | bytes 13641974 | solution.py:120
  208.1 1.2 dynamic-slice_bitcast_fusion.3
  209.3 6.1 %while.22 = (s32[]{:T(128)}, bf16[3,512,128]{2,1,0:T(8,128)(2,1)S(1)}, bf16[3,512,128]{2,1,0:T(8,128)(2,1)S(1)}, bf16[1536,128]{1,0:T(8,128)(2,1)S(1)}, bf16[1536,128]{1,0:T(8,128)(2,1)S(1)}, /*index=5*/s32[]{:T(128)}) while((s32[]{:T(128)}, bf16[3,512,128]{2,1,0:T(8,128)(2,1)S(1)}, bf16[3,512,128]{2,1,0:T(8,128)(2,1)S(1)}, ...), condition=%wide.region_4.4_spmd, body=%wide.region_1.3_spmd.sunk | while | flops 408222720 | bytes 10496085 | solution.py:52
  216.1 1.2 dynamic-slice_bitcast_fusion.3
  217.3 6.1 %while.22 = (s32[]{:T(128)}, bf16[3,512,128]{2,1,0:T(8,128)(2,1)S(1)}, bf16[3,512,128]{2,1,0:T(8,128)(2,1)S(1)}, bf16[1536,128]{1,0:T(8,128)(2,1)S(1)}, bf16[1536,128]{1,0:T(8,128)(2,1)S(1)}, /*index=5*/s32[]{:T(128)}) while((s32[]{:T(128)}, bf16[3,512,128]{2,1,0:T(8,128)(2,1)S(1)}, bf16[3,512,128]{2,1,0:T(8,128)(2,1)S(1)}, ...), condition=%wide.region_4.4_spmd, body=%wide.region_1.3_spmd.sunk | while | flops 408222720 | bytes 10496085 | solution.py:52
  223.4 0.8 bitcast_dynamic-update-slice_fusion.2
  224.2 1.2 dynamic-slice_bitcast_fusion.3
  225.4 6.1 %while.22 = (s32[]{:T(128)}, bf16[3,512,128]{2,1,0:T(8,128)(2,1)S(1)}, bf16[3,512,128]{2,1,0:T(8,128)(2,1)S(1)}, bf16[1536,128]{1,0:T(8,128)(2,1)S(1)}, bf16[1536,128]{1,0:T(8,128)(2,1)S(1)}, /*index=5*/s32[]{:T(128)}) while((s32[]{:T(128)}, bf16[3,512,128]{2,1,0:T(8,128)(2,1)S(1)}, bf16[3,512,128]{2,1,0:T(8,128)(2,1)S(1)}, ...), condition=%wide.region_4.4_spmd, body=%wide.region_1.3_spmd.sunk | while | flops 408222720 | bytes 10496085 | solution.py:52
  232.2 8.1 %copy.201 = bf16[3,1536,128]{2,0,1:T(4,128)(2,1)} copy(bf16[3,1536,128]{2,1,0:T(8,128)(2,1)} %get-tuple-element.56) | data formatting | bytes 2359296 | tf_op jit(solution)/shard_map/while | solution.py:120
  240.3 5.4 all-to-all-start.3
  245.9 74.3 %all-to-all-done.3 = bf16[1,3,1536,128]{3,1,0,2:T(4,128)(2,1)S(1)} async-done(((bf16[1,3,1536,128]{3,1,0,2:T(4,128)(2,1)}), bf16[1,3,1536,128]{3,1,0,2:T(4,128)(2,1)S(1)}, u32[]{:S(2)}, u32[]{:S(2)}) %all-to-all-start.3) | async-done | bytes 1179680 | tf_op jit(solution)/shard_map/all_to_all | solution.py:121
  320.6 3.1 fusion.19
  323.9 22.0 %multiply_reduce_fusion = f32[32,48]{1,0:T(8,128)S(1)} fusion(bf16[1,3,32,48,128]{4,1,3,2,0:T(4,128)(2,1)S(1)} %bitcast.345, f32[32,48]{1,0:T(8,128)S(1)} %broadcast_bitcast_fusion.2), kind=kLoop, calls=%fused_computation.17 | loop fusion | flops 2357760 | bytes 1191936 | tf_op jit(solution)/shard_map/reduce_sum | solution.py:127
  346.0 1.6 fusion.28
  349.4 37.0 %all_gather.3 = bf16[64,3,2,512]{3,2,1,0:T(2,128)(2,1)S(1)} all-gather(bf16[4,3,2,512]{3,2,1,0:T(2,128)(2,1)S(1)} %get-tuple-element.79), channel_id=1, replica_groups=mesh['sec'=2,'seq'=32,'rep'=8] {'sec','rep'}, dimensions={0}, use_global_device_ids=true | all-gather | bytes 417792 | tf_op jit(solution)/shard_map/all_gather | solution.py:142
  387.2 5.2 collective-permute-start
  392.3 1.5 collective-permute-start.1
  394.0 4.1 collective-permute-done.1
  418.2 7.9 %copy.183 = bf16[4,3,2,32,27,16]{3,2,1,0,5,4:T(2,128)(2,1)S(1)} copy(bf16[4,3,2,32,27,16]{5,3,2,1,0,4:T(8,128)(2,1)} %fusion.49) | data formatting | bytes 1327104 | tf_op jit(solution)/shard_map/stack | solution.py:80
  426.1 2.5 reshape_reshape.3
  428.6 1.7 convolution_add_fusion
  430.3 1.6 copy.184
  431.9 2.5 reshape.112
  434.4 2.7 reshape.113
  437.7 61.4 %psum.14 = f32[4,32]{1,0:T(4,128)S(1)} all-reduce(f32[4,32]{1,0:T(4,128)S(1)} %copy.185), channel_id=1, replica_groups=mesh['sec'=2,'seq'=32,'rep'=8] {'seq'}, use_global_device_ids=true, to_apply=%region_11.12 | all-reduce | flops 128 | bytes 1024 | tf_op jit(solution)/shard_map/psum | solution.py:154
  500.0 60.8 %psum.15 = f32[4,32]{1,0:T(4,128)S(1)} all-reduce(f32[4,32]{1,0:T(4,128)S(1)} %copy.187), channel_id=1, replica_groups=mesh['sec'=2,'seq'=32,'rep'=8] {'seq'}, use_global_device_ids=true, to_apply=%region_13.14 | all-reduce | flops 128 | bytes 1024 | tf_op jit(solution)/shard_map/psum | solution.py:156
  561.2 2.5 mul.94
  564.0 2.5 sub.70
  566.5 4.5 fusion.20
  (133 shorter events, 48.4 us)
Async XLA Ops:
  0.6 428.0 %copy-start = (bf16[3,3,3,16,512]{4,3,2,1,0:T(8,128)(2,1)S(1)}, bf16[3,3,3,16,512]{4,3,2,1,0:T(8,128)(2,1)}, u32[]{:S(2)}) copy-start(bf16[3,3,3,16,512]{4,3,2,1,0:T(8,128)(2,1)} %param.28) | copy-start | bytes 1327108
  0.6 75.7 %all-to-all-start = ((bf16[32,3,48,128]{3,2,1,0:T(8,128)(2,1)}), bf16[32,3,48,128]{3,2,1,0:T(8,128)(2,1)S(1)}, u32[]{:S(2)}, u32[]{:S(2)}) async-start(bf16[32,3,48,128]{3,2,1,0:T(8,128)(2,1)} %bitcast.385), calls=%async_computation | async-start | bytes 2359296 | tf_op jit(solution)/shard_map/all_to_all | solution.py:114
  142.7 63.0 %all-to-all-start.2 = ((bf16[32,3,48,128]{3,2,1,0:T(8,128)(2,1)}), bf16[32,3,48,128]{3,2,1,0:T(8,128)(2,1)}, u32[]{:S(2)}, u32[]{:S(2)}) async-start(bf16[32,3,48,128]{3,2,1,0:T(8,128)(2,1)} %bitcast.386), calls=%async_computation.2 | async-start | bytes 2359296 | tf_op jit(solution)/shard_map/all_to_all | solution.py:119
  240.3 5.4 copy-start.6
  240.3 5.5 copy-start.9
  240.3 5.6 copy-start.4
  240.3 5.6 copy-start.1
  240.3 5.6 copy-start.2
  240.3 79.9 %all-to-all-start.3 = ((bf16[1,3,1536,128]{3,1,0,2:T(4,128)(2,1)}), bf16[1,3,1536,128]{3,1,0,2:T(4,128)(2,1)S(1)}, u32[]{:S(2)}, u32[]{:S(2)}) async-start(bf16[1,3,1536,128]{3,1,0,2:T(4,128)(2,1)} %bitcast.350), calls=%async_computation.3 | async-start | bytes 3145728 | tf_op jit(solution)/shard_map/all_to_all | solution.py:121
  323.9 22.1 %copy-start.7 = (bf16[3072,64]{0,1:T(8,128)(2,1)S(1)}, bf16[3072,64]{0,1:T(8,128)(2,1)}, u32[]{:S(2)}) copy-start(bf16[3072,64]{0,1:T(8,128)(2,1)} %param.23) | copy-start | bytes 1179652
  323.9 22.1 %copy-start.10 = (f32[64]{0:T(128)S(1)}, f32[64]{0:T(128)}, u32[]{:S(2)}) copy-start(f32[64]{0:T(128)} %param.24) | copy-start | bytes 772
  347.6 1.1 copy-start.3
  347.6 46.3 %copy-start.5 = (f32[512]{0:T(512)S(1)}, f32[512]{0:T(512)}, u32[]{:S(2)}) copy-start(f32[512]{0:T(512)} %param.30) | copy-start | bytes 6148
  387.2 6.8 %collective-permute-start = (bf16[4,3,1,512]{3,2,1,0:T(2,128)(2,1)S(1)}, bf16[4,3,1,512]{3,2,1,0:T(2,128)(2,1)S(1)}, u32[]{:S(2)}, u32[]{:S(2)}) collective-permute-start(bf16[4,3,1,512]{3,2,1,0:T(2,128)(2,1)S(1)} %get-tuple-element.89), channel_id=1, source_target_pairs={{0,8},{8,16},{16,24},{24,32},{32,40},{40,48},{48,56},{56,64},{64,7... | collective-permute-start | bytes 36872 | tf_op jit(solution)/shard_map/ppermute | solution.py:29
  392.3 5.7 %collective-permute-start.1 = (bf16[4,3,1,512]{3,2,1,0:T(2,128)(2,1)S(1)}, bf16[4,3,1,512]{3,2,1,0:T(2,128)(2,1)S(1)}, u32[]{:S(2)}, u32[]{:S(2)}) collective-permute-start(bf16[4,3,1,512]{3,2,1,0:T(2,128)(2,1)S(1)} %get-tuple-element.90), channel_id=1, source_target_pairs={{8,0},{16,8},{24,16},{32,24},{40,32},{48,40},{56,48},{64,56},{72,6... | collective-permute-start | bytes 36872 | tf_op jit(solution)/shard_map/ppermute | solution.py:31
  426.1 2.5 copy-start.8
